TPU v7x, 32 devices: a whole 2x2x4 slice. The times are simulated.
32 devices in a mesh: gx: 8 (over z, y), gy: 4 (over x, core).
Axes of the slice: x: 2, y: 2, z: 4, core: 2. Of those that a mesh axis runs over, the one named last changes fastest.
Arguments:
- conc_prev: float32 [128, 64, 128], P('gx', 'gy'), may hold values from 0.5 to 2
- right_side: float32 [128, 64, 128], P('gx', 'gy'), may hold values from -5 to 7
- soil_id: int32 [128, 64, 128], P('gx', 'gy'), may hold values from 0 to 7
- soil_table: float32 [5, 8], replicated, may hold values from 0.3 to 3
Outputs:
- correction: float32 [128, 64, 128], P('gx', 'gy')
All inputs are finite; a program needn't handle non-finite values.
Results may differ from a plain program's by a relative error of at most 0.00002.
Values sent between devices are 32-bit elements; how exact they have to be, the bound alone decides.
No kernel may reach another device: no remote copies, remote signals or barrier semaphores. Data moves between devices by JAX's collectives and lax.ppermute only.
A program may use at most 128 MiB of HBM per device.

v0:
```python
import jax
import jax.numpy as jnp
from jax import lax
from jax.sharding import PartitionSpec as P

CHEB = 3
COARSE_SWEEPS = 8
storage_scale = 0.05
cheb_centre = 1.1
cheb_half = 0.9
cheb_ratio = cheb_centre / cheb_half
jacobi_weight = 0.8
FINE_HALO = 10
MID_HALO = 5
HIGH = lax.Precision.HIGHEST


def shift_from(cells, axis, offset):
    count = lax.axis_size(axis)
    if offset > 0:
        pairs = [(i + offset, i) for i in range(count - offset)]
    else:
        pairs = [(i, i - offset) for i in range(count + offset)]
    if not pairs:
        return jnp.zeros_like(cells)
    return lax.ppermute(cells, axis, pairs)


def halo(cells, sides, width):
    for axis, dim in sides:
        size = cells.shape[dim]
        head = lax.slice_in_dim(cells, 0, width, axis=dim)
        tail = lax.slice_in_dim(cells, size - width, size, axis=dim)
        cells = jnp.concatenate(
            [shift_from(tail, axis, -1), cells, shift_from(head, axis, 1)], axis=dim
        )
    return cells


def harmonic(first, second):
    return first * second / jnp.maximum(0.5 * (first + second), 0.1)


def win(a, n, margin, r, dx=0, dy=0):
    lo = margin - r
    hi = margin + n + r
    return a[..., lo + dx : hi + dx, lo + dy : hi + dy, :]


def pair_matrix(size, dtype=jnp.float32):
    rows = jnp.arange(size)[:, None] // 2
    cols = jnp.arange(size // 2)[None, :]
    return (rows == cols).astype(dtype)


def coarsen(values):
    lead = values.shape[:-3]
    sx, sy, sz = values.shape[-3:]
    v = values.reshape(lead + (sx // 2, 2, sy, sz))
    v = v[..., 0, :, :] + v[..., 1, :, :]
    v = jnp.einsum("...yz,zw->...yw", v, pair_matrix(sz), precision=HIGH)
    v = jnp.einsum("...yw,yv->...vw", v, pair_matrix(sy), precision=HIGH)
    return v * 0.125


def prolong(values):
    sx, sy, sz = values.shape
    v = jnp.einsum("xyz,wz->xyw", values, pair_matrix(2 * sz), precision=HIGH)
    v = jnp.einsum("xyw,vy->xvw", v, pair_matrix(2 * sy), precision=HIGH)
    v = jnp.broadcast_to(v[:, None], (sx, 2) + v.shape[1:]).reshape((2 * sx,) + v.shape[1:])
    return v


def build_level(coeffs, n, margin, spacing):
    kx, ky, kz, store = (coeffs[0], coeffs[1], coeffs[2], coeffs[3])
    fx = harmonic(kx[1:], kx[:-1]) * spacing
    fy = harmonic(ky[:, 1:], ky[:, :-1]) * spacing
    vertical = harmonic(kz[:, :, 1:], kz[:, :, :-1]) * spacing
    closed = jnp.zeros_like(kz[:, :, :1])
    above = jnp.concatenate([vertical, closed], axis=2)
    below = jnp.concatenate([closed, vertical], axis=2)
    level = dict(n=n, m=margin, fx=fx, fy=fy, above=above, below=below, store=store)
    r = margin - 1
    level["diag"] = jnp.maximum(faces_sum(level, r) + win(store, n, margin, r), 0.01)
    level["dm"] = r
    return level


def faces_sum(level, r):
    n, m = (level["n"], level["m"])
    east = win(level["fx"], n, m, r)
    west = win(level["fx"], n, m, r, dx=-1)
    north = win(level["fy"], n, m, r)
    south = win(level["fy"], n, m, r, dy=-1)
    above = win(level["above"], n, m, r)
    below = win(level["below"], n, m, r)
    return east + west + north + south + above + below


def operate(values, vm, level):
    n, m = (level["n"], level["m"])
    r = vm - 1
    centre = win(values, n, vm, r)
    upper = jnp.concatenate([centre[:, :, 1:], centre[:, :, :1]], axis=2)
    lower = jnp.concatenate([centre[:, :, -1:], centre[:, :, :-1]], axis=2)
    fx, fy = (level["fx"], level["fy"])
    fluxes = win(fx, n, m, r) * (centre - win(values, n, vm, r, dx=1))
    fluxes = fluxes + win(fx, n, m, r, dx=-1) * (centre - win(values, n, vm, r, dx=-1))
    fluxes = fluxes + win(fy, n, m, r) * (centre - win(values, n, vm, r, dy=1))
    fluxes = fluxes + win(fy, n, m, r, dy=-1) * (centre - win(values, n, vm, r, dy=-1))
    fluxes = fluxes + win(level["above"], n, m, r) * (centre - upper)
    fluxes = fluxes + win(level["below"], n, m, r) * (centre - lower)
    return win(level["store"], n, m, r) * centre + fluxes


def chebyshev(target, tm, initial, im, level):
    n = level["n"]
    diag, dm = (level["diag"], level["dm"])
    if initial is None:
        cur = min(tm, dm)
        misfit = win(target, n, tm, cur)
        update = misfit / win(diag, n, dm, cur) * (1.0 / cheb_centre)
        iterate = update
    else:
        applied = operate(initial, im, level)
        cur = im - 1
        misfit = win(target, n, tm, cur) - applied
        update = misfit / win(diag, n, dm, cur) * (1.0 / cheb_centre)
        iterate = win(initial, n, im, cur) + update
    factor = 1.0 / cheb_ratio
    for repeat in range(CHEB - 1):
        applied = operate(iterate, cur, level)
        nxt = cur - 1
        misfit = win(target, n, tm, nxt) - applied
        factor_new = 1.0 / (2.0 * cheb_ratio - factor)
        update = factor_new * factor * win(update, n, cur, nxt) + 2.0 * factor_new / cheb_half * (
            misfit / win(diag, n, dm, nxt)
        )
        iterate = win(iterate, n, cur, nxt) + update
        cur = nxt
        factor = factor_new
    return (iterate, cur)


def lookup(soil_id, soil_table, record):
    looked = jnp.full(soil_id.shape, soil_table[record, soil_table.shape[1] - 1])
    for material in range(soil_table.shape[1] - 2, -1, -1):
        looked = jnp.where(soil_id == material, soil_table[record, material], looked)
    return looked


def local(conc_prev, right_side, soil_id, soil_table):
    n = conc_prev.shape[0]
    ny = conc_prev.shape[1]
    hf = FINE_HALO
    gx_count = lax.axis_size("gx")
    gy_count = lax.axis_size("gy")
    ix = lax.axis_index("gx")
    iy = lax.axis_index("gy")
    stacked = jnp.stack([conc_prev, right_side, soil_id.astype(jnp.float32)])
    ext = halo(stacked, (("gx", 1), ("gy", 2)), hf)
    conc, rhs, idf = (ext[0], ext[1], ext[2])
    ids = idf.astype(jnp.int32)
    gxi = ix * n - hf + jnp.arange(n + 2 * hf)
    gyi = iy * ny - hf + jnp.arange(ny + 2 * hf)
    inside = ((gxi >= 0) & (gxi < gx_count * n))[:, None, None] & (
        (gyi >= 0) & (gyi < gy_count * ny)
    )[None, :, None]
    kx = jnp.where(inside, lookup(ids, soil_table, 0), 0.0)
    ky = jnp.where(inside, lookup(ids, soil_table, 1), 0.0)
    kz = jnp.where(inside, lookup(ids, soil_table, 2), 0.0)
    s3 = lookup(ids, soil_table, 3)
    s4 = lookup(ids, soil_table, 4)
    store = storage_scale * (1.0 + s3 * jnp.exp((s4 - 1.0) * jnp.log(conc)))
    store = jnp.where(inside, store, 0.0)
    fine_c = jnp.stack([kx, ky, kz, store])
    fine = build_level(fine_c, n, hf, 1.0)
    x0, x0m = chebyshev(rhs, hf, None, 0, fine)
    r0 = win(rhs, n, hf, x0m - 1) - operate(x0, x0m, fine)
    r0m = x0m - 1
    nm = n // 2
    mm = hf // 2
    mid_c = coarsen(fine_c)
    mid = build_level(mid_c, nm, mm, 0.25)
    b1 = coarsen(win(r0, n, r0m, 2 * (r0m // 2)))
    b1m = r0m // 2
    x1, x1m = chebyshev(b1, b1m, None, 0, mid)
    r1 = win(b1, nm, b1m, x1m - 1) - operate(x1, x1m, mid)
    r1m = x1m - 1
    b2 = coarsen(win(r1, nm, r1m, 0))
    coarse_own = coarsen(win(mid_c, nm, mm, 0))
    nc = b2.shape[0]
    reach = 2
    cpack = jnp.concatenate([b2[None], coarse_own], axis=0)
    cpack = lax.all_gather(cpack, "gy", axis=2, tiled=True)
    parts = [shift_from(cpack, "gx", -d) for d in range(reach, 0, -1)]
    parts += [cpack]
    parts += [shift_from(cpack, "gx", d) for d in range(1, reach + 1)]
    cpack = jnp.concatenate(parts, axis=1)
    cm = reach * nc
    source = cpack[0]
    cc = cpack[1:]
    line_total = jnp.sum(source, axis=1)
    line_store = jnp.sum(cc[3], axis=1)
    line_mean = jnp.where(
        line_store > 0, line_total / jnp.where(line_store > 0, line_store, 1.0), 0.0
    )
    width = source.shape[0]
    ccp = jnp.pad(cc, ((0, 0), (0, 0), (1, 1), (0, 0)))
    kx_, ky_, kz_, st_ = (ccp[0], ccp[1], ccp[2], ccp[3])
    q = 0.0625
    cx = kx_[1:-1, 1:-1]
    cy = ky_[1:-1, 1:-1]
    cz = kz_[1:-1, 1:-1]
    east = harmonic(kx_[2:, 1:-1], cx) * q
    west = harmonic(kx_[:-2, 1:-1], cx) * q
    north = harmonic(ky_[1:-1, 2:], cy) * q
    south = harmonic(ky_[1:-1, :-2], cy) * q
    vert = harmonic(cz[:, :, 1:], cz[:, :, :-1]) * q
    closed = jnp.zeros_like(cz[:, :, :1])
    above = jnp.concatenate([vert, closed], axis=2)
    below = jnp.concatenate([closed, vert], axis=2)
    cst = st_[1:-1, 1:-1]
    cdiag = jnp.maximum(cst + east + west + north + south + above + below, 0.01)
    csrc = source[1:-1]
    u = jnp.broadcast_to(line_mean[:, None, :], source.shape)
    for sweep in range(COARSE_SWEEPS):
        lo = sweep
        cur = u
        up = jnp.pad(cur, ((0, 0), (1, 1), (0, 0)))
        centre = up[1:-1, 1:-1]
        sl = slice(lo, width - 2 - lo)
        upper = jnp.concatenate([centre[:, :, 1:], centre[:, :, :1]], axis=2)
        lower = jnp.concatenate([centre[:, :, -1:], centre[:, :, :-1]], axis=2)
        fl = east[sl] * (centre - up[2:, 1:-1]) + west[sl] * (centre - up[:-2, 1:-1])
        fl = fl + north[sl] * (centre - up[1:-1, 2:]) + south[sl] * (centre - up[1:-1, :-2])
        fl = fl + above[sl] * (centre - upper) + below[sl] * (centre - lower)
        applied = cst[sl] * centre + fl
        u = centre + jacobi_weight * ((csrc[sl] - applied) / cdiag[sl])
    ncy = nc
    u = lax.dynamic_slice_in_dim(u, iy * ncy, ncy, 1)
    s1 = win(x1, nm, x1m, 0) + prolong(u)
    mpack = jnp.stack([s1, win(b1, nm, b1m, 0)])
    mpack = halo(mpack, (("gx", 1), ("gy", 2)), MID_HALO)
    s1e, b1e = (mpack[0], mpack[1])
    y1, y1m = chebyshev(b1e, MID_HALO, s1e, MID_HALO, mid)
    fm = 2 * y1m
    s0 = win(x0, n, x0m, fm) + prolong(y1)
    fs = min(fm, CHEB)
    s0 = win(s0, n, fm, fs)
    out, om = chebyshev(rhs, hf, s0, fs, fine)
    return out


def solution(mesh):
    placed = (P("gx", "gy", None), P("gx", "gy", None), P("gx", "gy", None), P())
    return jax.shard_map(
        local, mesh=mesh, in_specs=placed, out_specs=P("gx", "gy", None), check_vma=False
    )
```

profile of v0, /device:TPU:1, one launch (start us, length us, event | category | flops | bytes accessed | tf_op | source)
XLA Modules:
  0.0 162.3 jit_solution(11000969976232683504)
XLA Ops:
  0.0 1.0 fusion.164
  1.0 1.1 copy_bitcast_fusion
  2.1 4.0 %collective-permute-start = (f32[3,10,16,128]{3,1,2,0:T(8,128)S(1)}, f32[3,10,16,128]{3,1,2,0:T(8,128)S(1)}, u32[]{:S(2)}, u32[]{:S(2)}) collective-permute-start(f32[3,10,16,128]{3,1,2,0:T(8,128)S(1)} %get-tuple-element.62), channel_id=1, source_target_pairs={{0,4},{4,8},{8,12},{12,16},{16,20},{20,24},{24,28},{1,5},{5,9},{9,... | collective-permute-start | bytes 737288 | tf_op jit(solution)/shard_map/ppermute | solution.py:26
  6.1 1.3 collective-permute-start.1
  7.5 0.6 and_select_fusion
  8.0 0.5 and_select_fusion.4
  8.6 0.7 fusion.464
  9.2 13.1 %collective-permute-done = f32[3,10,16,128]{3,1,2,0:T(8,128)S(1)} collective-permute-done((f32[3,10,16,128]{3,1,2,0:T(8,128)S(1)}, f32[3,10,16,128]{3,1,2,0:T(8,128)S(1)}, u32[]{:S(2)}, u32[]{:S(2)}) %collective-permute-start) | collective-permute-done | bytes 245792 | tf_op jit(solution)/shard_map/ppermute | solution.py:26
  22.5 4.6 %collective-permute-start.2 = (f32[3,36,10,128]{3,1,2,0:T(8,128)S(1)}, f32[3,36,10,128]{3,1,2,0:T(8,128)S(1)}, u32[]{:S(2)}, u32[]{:S(2)}) collective-permute-start(f32[3,36,10,128]{3,1,2,0:T(8,128)S(1)} %get-tuple-element.37), channel_id=1, source_target_pairs={{0,1},{1,2},{2,3},{4,5},{5,6},{6,7},{8,9},{9,10},{10,11},{12,13},{... | collective-permute-start | bytes 1658888 | tf_op jit(solution)/shard_map/ppermute | solution.py:26
  27.1 1.9 %collective-permute-start.3 = (f32[3,36,10,128]{3,1,2,0:T(8,128)S(1)}, f32[3,36,10,128]{3,1,2,0:T(8,128)S(1)}, u32[]{:S(2)}, u32[]{:S(2)}) collective-permute-start(f32[3,36,10,128]{3,1,2,0:T(8,128)S(1)} %get-tuple-element.38), channel_id=1, source_target_pairs={{1,0},{2,1},{3,2},{5,4},{6,5},{7,6},{9,8},{10,9},{11,10},{13,12},{... | collective-permute-start | bytes 1658888 | tf_op jit(solution)/shard_map/ppermute | solution.py:26
  29.0 0.7 fusion.463
  29.7 0.7 fusion.462
  30.5 3.6 %collective-permute-done.2 = f32[3,36,10,128]{3,1,2,0:T(8,128)S(1)} collective-permute-done((f32[3,36,10,128]{3,1,2,0:T(8,128)S(1)}, f32[3,36,10,128]{3,1,2,0:T(8,128)S(1)}, u32[]{:S(2)}, u32[]{:S(2)}) %collective-permute-start.2) | collective-permute-done | bytes 552992 | tf_op jit(solution)/shard_map/ppermute | solution.py:26
  34.1 4.4 %collective-permute-done.3 = f32[3,36,10,128]{3,1,2,0:T(8,128)S(1)} collective-permute-done((f32[3,36,10,128]{3,1,2,0:T(8,128)S(1)}, f32[3,36,10,128]{3,1,2,0:T(8,128)S(1)}, u32[]{:S(2)}, u32[]{:S(2)}) %collective-permute-start.3) | collective-permute-done | bytes 552992 | tf_op jit(solution)/shard_map/ppermute | solution.py:26
  38.7 6.1 %broadcast_select_fusion.3 = (f32[1,36,36,128]{3,1,2,0:T(8,128)S(1)}, pred[1,36,36,128]{3,1,2,0:T(8,128)(4,1)S(1)}, pred[1,36,36,128]{3,1,2,0:T(8,128)(4,1)S(1)}...) fusion(pred[36,36]{0,1:T(8,128)(4,1)S(1)} %broadcast_and_fusion, ...), kind=kLoop, calls=%fused_computation.137 | loop fusion | flops 2654208 | bytes 3816752 | tf_op jit(solution)/shard_map/jit(_where)/select_n | solution.py:169
  44.8 5.5 %broadcast_select_fusion.2 = f32[1,36,36,128]{3,1,2,0:T(8,128)S(1)} fusion(pred[36,36]{0,1:T(8,128)(4,1)S(1)} %broadcast_and_fusion, pred[1,36,36,128]{3,1,2,0:T(8,128)(4,1)S(1)} %get-tuple-element.33, pred[1,36,36,128]{3,1,2,0:T(8,128)(4,1)S(1)} %get-tuple-element.32, pred[1,36,36,128]{3,1,2,0:T(8,128)(4,1)S(1)} %get-tuple-element.31, ...), kind=kLoop, calls=%fused_computation.136 | loop fusion | flops 1327104 | bytes 1826096 | tf_op jit(solution)/shard_map/jit(_where)/select_n | solution.py:170
  50.3 5.5 %bitcast_select_fusion.2 = f32[36,36,128]{2,0,1:T(8,128)S(1)} fusion(pred[36,36]{0,1:T(8,128)(4,1)S(1)} %broadcast_and_fusion, pred[1,36,36,128]{3,1,2,0:T(8,128)(4,1)S(1)} %get-tuple-element.33, pred[1,36,36,128]{3,1,2,0:T(8,128)(4,1)S(1)} %get-tuple-element.32, pred[1,36,36,128]{3,1,2,0:T(8,128)(4,1)S(1)} %get-tuple-element.31, ...), kind=kLoop, calls=%fused_computation.31 | loop fusion | flops 1327104 | bytes 1826096 | tf_op jit(solution)/shard_map/jit(_where)/select_n | solution.py:170
  55.8 5.7 %broadcast_select_fusion.1 = f32[1,36,36,128]{3,1,2,0:T(8,128)S(1)} fusion(pred[36,36]{0,1:T(8,128)(4,1)S(1)} %broadcast_and_fusion, pred[1,36,36,128]{3,1,2,0:T(8,128)(4,1)S(1)} %get-tuple-element.33, pred[1,36,36,128]{3,1,2,0:T(8,128)(4,1)S(1)} %get-tuple-element.32, pred[1,36,36,128]{3,1,2,0:T(8,128)(4,1)S(1)} %get-tuple-element.31, ...), kind=kLoop, calls=%fused_computation.135 | loop fusion | flops 1327104 | bytes 1826096 | tf_op jit(solution)/shard_map/jit(_where)/select_n | solution.py:171
  61.5 5.7 %bitcast_select_fusion.1 = f32[36,36,128]{2,0,1:T(8,128)S(1)} fusion(pred[36,36]{0,1:T(8,128)(4,1)S(1)} %broadcast_and_fusion, pred[1,36,36,128]{3,1,2,0:T(8,128)(4,1)S(1)} %get-tuple-element.33, pred[1,36,36,128]{3,1,2,0:T(8,128)(4,1)S(1)} %get-tuple-element.32, pred[1,36,36,128]{3,1,2,0:T(8,128)(4,1)S(1)} %get-tuple-element.31, ...), kind=kLoop, calls=%fused_computation.30 | loop fusion | flops 1327104 | bytes 1826096 | tf_op jit(solution)/shard_map/jit(_where)/select_n | solution.py:171
  67.3 0.7 copy.30
  68.0 11.0 %broadcast_select_fusion = (f32[1,36,36,128]{3,1,2,0:T(8,128)S(1)}, f32[1,36,36,128]{3,1,2,0:T(8,128)S(1)}) fusion(pred[36,36]{0,1:T(8,128)(4,1)S(1)} %broadcast_and_fusion, f32[3,36,36,128]{3,1,2,0:T(8,128)S(1)} %pad_maximum_fusion.1, pred[1,36,36,128]{3,1,2,0:T(8,128)(4,1)S(1)} %get-tuple-element.33, pred[1,36,36,128]{3,1,2,0:T(8,128)(4,1)S(1)} %get-tuple-element.32, ...), kind=kLoop, calls=%fused_computation.134 | loop fusion | flops 3317760 | bytes 3153232 | tf_op jit(solution)/shard_map/jit(_where)/select_n | solution.py:175
  79.0 0.7 copy.33
  79.7 0.7 copy.31
  80.4 0.7 copy.32
  81.1 2.7 %pad_maximum_fusion = f32[4,18,2,36,128]{4,0,3,2,1:T(4,128)S(1)} fusion(f32[1,18,2,36,128]{4,0,3,2,1:T(1,128)S(1)} %bitcast.252, f32[1,18,2,36,128]{4,0,3,2,1:T(1,128)S(1)} %bitcast.254, f32[1,18,2,36,128]{4,0,3,2,1:T(1,128)S(1)} %bitcast.253, f32[1,18,2,36,128]{4,0,3,2,1:T(1,128)S(1)} %bitcast.251), kind=kLoop, calls=%fused_computation | loop fusion | flops 1990656 | bytes 5308416 | tf_op jit(solution)/shard_map/stack | solution.py:176
  83.8 0.3 fusion.2
  84.2 0.8 fusion
  85.0 0.7 fusion.3
  85.7 0.7 multiply_bitcast_fusion
  86.4 0.7 slice_bitcast_fusion.4
  87.3 5.6 %bitcast_select_fusion.3 = (f32[36,36,128]{2,0,1:T(8,128)S(1)}, f32[36,36,128]{2,0,1:T(8,128)S(1)}) fusion(pred[36,36]{0,1:T(8,128)(4,1)S(1)} %broadcast_and_fusion, pred[1,36,36,128]{3,1,2,0:T(8,128)(4,1)S(1)} %get-tuple-element.33, pred[1,36,36,128]{3,1,2,0:T(8,128)(4,1)S(1)} %get-tuple-element.32, pred[1,36,36,128]{3,1,2,0:T(8,128)(4,1)S(1)} %get-tuple-element.31, ...), kind=kLoop, calls=%fused_computation.32 | loop fusion | flops 1492992 | bytes 3153200 | tf_op jit(solution)/shard_map/jit(_where)/select_n | solution.py:169
  93.1 0.3 maximum_divide_fusion
  93.4 0.8 fusion.15
  94.6 1.2 slice_add_fusion.5
  96.2 1.1 fusion.33
  97.8 0.8 divide_multiply_fusion
  98.6 0.8 divide_multiply_fusion.1
  99.4 1.7 %fusion.58 = f32[28,28,128]{2,0,1:T(8,128)} fusion(f32[36,36,127]{2,0,1:T(8,128)S(1)} %maximum_divide_fusion, f32[30,30,128]{2,0,1:T(8,128)S(1)} %fusion.33, f32[36,35,128]{2,0,1:T(8,128)S(1)} %maximum_divide_fusion.2, f32[35,36,128]{2,0,1:T(8,128)S(1)} %maximum_divide_fusion.1, f32[36,36,128]{2,0,1:T(8,128)S(1)} %get-tuple-element.151, ...), kind=kLoop, calls=%fused_computation.116 | loop fusion | flops 2207744 | bytes 6278080 | tf_op jit(solution)/shard_map/sub | solution.py:179
  101.1 2.0 %reshape.377 = f32[14,2,28,128]{3,1,0,2:T(2,128)} reshape(f32[28,28,128]{2,0,1:T(8,128)} %fusion.58) | data formatting | bytes 802816 | tf_op jit(solution)/shard_map/reshape | solution.py:59
  103.1 1.5 fusion.426
  104.6 0.9 fusion.87
  105.5 1.5 add_maximum_fusion.1
  109.1 4.4 %all_gather.3 = f32[5,4,16,32]{3,1,0,2:T(4,128)S(1)} all-gather(f32[5,4,4,32]{3,1,0,2:T(4,128)S(1)} %copy.39), channel_id=1, replica_groups=mesh['gx'=8,'gy'=4] {'gy'}, dimensions={2}, use_global_device_ids=true | all-gather | bytes 51200 | tf_op jit(solution)/shard_map/all_gather | solution.py:195
  113.4 5.1 %collective-permute-start.4 = (f32[5,4,16,32]{3,2,1,0:T(8,128)S(1)}, f32[5,4,16,32]{3,2,1,0:T(8,128)S(1)}, u32[]{:S(2)}, u32[]{:S(2)}) collective-permute-start(f32[5,4,16,32]{3,2,1,0:T(8,128)S(1)} %copy.40), channel_id=1, source_target_pairs={{0,8},{4,12},{8,16},{12,20},{16,24},{20,28},{1,9},{5,13},{9,17},{1... | collective-permute-start | bytes 122888 | tf_op jit(solution)/shard_map/ppermute | solution.py:26
  118.5 1.3 collective-permute-start.7
  119.8 1.3 collective-permute-start.6
  121.1 4.2 %collective-permute-start.5 = (f32[5,4,16,32]{3,2,1,0:T(8,128)S(1)}, f32[5,4,16,32]{3,2,1,0:T(8,128)S(1)}, u32[]{:S(2)}, u32[]{:S(2)}) collective-permute-start(f32[5,4,16,32]{3,2,1,0:T(8,128)S(1)} %copy.40), channel_id=1, source_target_pairs={{0,4},{4,8},{8,12},{12,16},{16,20},{20,24},{24,28},{1,5},{5,9},{9,... | collective-permute-start | bytes 122888 | tf_op jit(solution)/shard_map/ppermute | solution.py:26
  125.4 6.0 %collective-permute-done.5 = f32[5,4,16,32]{3,2,1,0:T(8,128)S(1)} collective-permute-done((f32[5,4,16,32]{3,2,1,0:T(8,128)S(1)}, f32[5,4,16,32]{3,2,1,0:T(8,128)S(1)}, u32[]{:S(2)}, u32[]{:S(2)}) %collective-permute-start.5) | collective-permute-done | bytes 40992 | tf_op jit(solution)/shard_map/ppermute | solution.py:26
  132.5 0.4 multiply_add_fusion
  135.8 4.1 %collective-permute-start.8 = (f32[2,5,8,64]{3,2,1,0:T(8,128)S(1)}, f32[2,5,8,64]{3,2,1,0:T(8,128)S(1)}, u32[]{:S(2)}, u32[]{:S(2)}) collective-permute-start(f32[2,5,8,64]{3,2,1,0:T(8,128)S(1)} %get-tuple-element.135), channel_id=1, source_target_pairs={{0,4},{4,8},{8,12},{12,16},{16,20},{20,24},{24,28},{1,5},{5,9},{9,... | collective-permute-start | bytes 61448 | tf_op jit(solution)/shard_map/ppermute | solution.py:26
  140.0 1.3 collective-permute-start.9
  141.3 3.4 %collective-permute-done.9 = f32[2,5,8,64]{3,2,1,0:T(8,128)S(1)} collective-permute-done((f32[2,5,8,64]{3,2,1,0:T(8,128)S(1)}, f32[2,5,8,64]{3,2,1,0:T(8,128)S(1)}, u32[]{:S(2)}, u32[]{:S(2)}) %collective-permute-start.9) | collective-permute-done | bytes 20512 | tf_op jit(solution)/shard_map/ppermute | solution.py:26
  144.7 5.6 %collective-permute-start.10 = (f32[2,18,5,64]{3,2,1,0:T(8,128)S(1)}, f32[2,18,5,64]{3,2,1,0:T(8,128)S(1)}, u32[]{:S(2)}, u32[]{:S(2)}) collective-permute-start(f32[2,18,5,64]{3,2,1,0:T(8,128)S(1)} %get-tuple-element.91), channel_id=1, source_target_pairs={{0,1},{1,2},{2,3},{4,5},{5,6},{6,7},{8,9},{9,10},{10,11},{12,13},{... | collective-permute-start | bytes 138248 | tf_op jit(solution)/shard_map/ppermute | solution.py:26
  150.4 1.9 %collective-permute-start.11 = (f32[2,18,5,64]{3,2,1,0:T(8,128)S(1)}, f32[2,18,5,64]{3,2,1,0:T(8,128)S(1)}, u32[]{:S(2)}, u32[]{:S(2)}) collective-permute-start(f32[2,18,5,64]{3,2,1,0:T(8,128)S(1)} %get-tuple-element.92), channel_id=1, source_target_pairs={{1,0},{2,1},{3,2},{5,4},{6,5},{7,6},{9,8},{10,9},{11,10},{13,12},{... | collective-permute-start | bytes 138248 | tf_op jit(solution)/shard_map/ppermute | solution.py:26
  152.4 4.4 %collective-permute-done.11 = f32[2,18,5,64]{3,2,1,0:T(8,128)S(1)} collective-permute-done((f32[2,18,5,64]{3,2,1,0:T(8,128)S(1)}, f32[2,18,5,64]{3,2,1,0:T(8,128)S(1)}, u32[]{:S(2)}, u32[]{:S(2)}) %collective-permute-start.11) | collective-permute-done | bytes 46112 | tf_op jit(solution)/shard_map/ppermute | solution.py:26
  157.2 0.3 slice_add_fusion.9
  157.7 0.3 slice_add_fusion.10
  158.2 0.4 fusion.222
  158.6 0.3 convolution_bitcast_fusion
  159.4 0.3 copy-done.1
  159.9 0.4 slice_add_fusion.7
  160.6 0.5 slice_add_fusion.8
  161.3 0.3 fusion.144
  161.7 0.7 copy.48
  (136 shorter events, 9.9 us)
Async XLA Ops:
  0.0 8.6 %copy-start.8 = (f32[5,8]{1,0:T(8,128)S(1)}, f32[5,8]{1,0:T(8,128)}, u32[]{:S(2)}) copy-start(f32[5,8]{1,0:T(8,128)} %param.7) | copy-start | bytes 484
  2.1 20.2 %collective-permute-start = (f32[3,10,16,128]{3,1,2,0:T(8,128)S(1)}, f32[3,10,16,128]{3,1,2,0:T(8,128)S(1)}, u32[]{:S(2)}, u32[]{:S(2)}) collective-permute-start(f32[3,10,16,128]{3,1,2,0:T(8,128)S(1)} %get-tuple-element.62), channel_id=1, source_target_pairs={{0,4},{4,8},{8,12},{12,16},{16,20},{20,24},{24,28},{1,5},{5,9},{9,... | collective-permute-start | bytes 737288 | tf_op jit(solution)/shard_map/ppermute | solution.py:26
  6.1 16.2 %collective-permute-start.1 = (f32[3,10,16,128]{3,1,2,0:T(8,128)S(1)}, f32[3,10,16,128]{3,1,2,0:T(8,128)S(1)}, u32[]{:S(2)}, u32[]{:S(2)}) collective-permute-start(f32[3,10,16,128]{3,1,2,0:T(8,128)S(1)} %get-tuple-element.63), channel_id=1, source_target_pairs={{4,0},{8,4},{12,8},{16,12},{20,16},{24,20},{28,24},{5,1},{9,5},{13... | collective-permute-start | bytes 737288 | tf_op jit(solution)/shard_map/ppermute | solution.py:26
  7.4 76.7 %copy-start.9 = (s32[128]{0:T(128)}, s32[128]{0:T(128)S(1)}, u32[]{:S(2)}) copy-start(s32[128]{0:T(128)S(1)} %and_select_fusion.3) | copy-start | bytes 1540
  22.5 11.6 %collective-permute-start.2 = (f32[3,36,10,128]{3,1,2,0:T(8,128)S(1)}, f32[3,36,10,128]{3,1,2,0:T(8,128)S(1)}, u32[]{:S(2)}, u32[]{:S(2)}) collective-permute-start(f32[3,36,10,128]{3,1,2,0:T(8,128)S(1)} %get-tuple-element.37), channel_id=1, source_target_pairs={{0,1},{1,2},{2,3},{4,5},{5,6},{6,7},{8,9},{9,10},{10,11},{12,13},{... | collective-permute-start | bytes 1658888 | tf_op jit(solution)/shard_map/ppermute | solution.py:26
  27.1 11.5 %collective-permute-start.3 = (f32[3,36,10,128]{3,1,2,0:T(8,128)S(1)}, f32[3,36,10,128]{3,1,2,0:T(8,128)S(1)}, u32[]{:S(2)}, u32[]{:S(2)}) collective-permute-start(f32[3,36,10,128]{3,1,2,0:T(8,128)S(1)} %get-tuple-element.38), channel_id=1, source_target_pairs={{1,0},{2,1},{3,2},{5,4},{6,5},{7,6},{9,8},{10,9},{11,10},{13,12},{... | collective-permute-start | bytes 1658888 | tf_op jit(solution)/shard_map/ppermute | solution.py:26
  92.9 6.5 %copy-start = (f32[36,36,128]{2,0,1:T(8,128)}, f32[36,36,128]{2,0,1:T(8,128)S(1)}, u32[]{:S(2)}) copy-start(f32[36,36,128]{2,0,1:T(8,128)S(1)} %get-tuple-element.151) | copy-start | bytes 1990660
  94.1 2.1 %copy-start.5 = (f32[34,34,128]{2,0,1:T(8,128)}, f32[34,34,128]{2,0,1:T(8,128)S(1)}, u32[]{:S(2)}) copy-start(f32[34,34,128]{2,0,1:T(8,128)S(1)} %get-tuple-element.25) | copy-start | bytes 1775620
  103.1 4.0 %copy-start.12 = (s32[28]{0:T(128)S(1)}, s32[28]{0:T(128)}, u32[]{:S(2)}) copy-start(s32[28]{0:T(128)} %and_select_fusion.4) | copy-start | bytes 340
  103.1 4.4 %copy-start.2 = (f32[18,18,63]{2,1,0:T(8,128)S(1)}, f32[18,18,63]{2,1,0:T(8,128)}, u32[]{:S(2)}) copy-start(f32[18,18,63]{2,1,0:T(8,128)} %divide_multiply_fusion) | copy-start | bytes 244948
  103.1 4.4 %copy-start.3 = (f32[17,18,64]{2,1,0:T(8,128)S(1)}, f32[17,18,64]{2,1,0:T(8,128)}, u32[]{:S(2)}) copy-start(f32[17,18,64]{2,1,0:T(8,128)} %multiply_bitcast_fusion) | copy-start | bytes 235012
  103.1 4.4 %copy-start.4 = (f32[18,17,64]{2,1,0:T(8,128)S(1)}, f32[18,17,64]{2,1,0:T(8,128)}, u32[]{:S(2)}) copy-start(f32[18,17,64]{2,1,0:T(8,128)} %divide_multiply_fusion.1) | copy-start | bytes 235012
  103.1 4.4 %copy-start.7 = (f32[18,18,64]{2,1,0:T(8,128)S(1)}, f32[18,18,64]{2,1,0:T(8,128)}, u32[]{:S(2)}) copy-start(f32[18,18,64]{2,1,0:T(8,128)} %get-tuple-element.40) | copy-start | bytes 248836
  107.5 0.8 copy-start.11
  113.4 11.9 %collective-permute-start.4 = (f32[5,4,16,32]{3,2,1,0:T(8,128)S(1)}, f32[5,4,16,32]{3,2,1,0:T(8,128)S(1)}, u32[]{:S(2)}, u32[]{:S(2)}) collective-permute-start(f32[5,4,16,32]{3,2,1,0:T(8,128)S(1)} %copy.40), channel_id=1, source_target_pairs={{0,8},{4,12},{8,16},{12,20},{16,24},{20,28},{1,9},{5,13},{9,17},{1... | collective-permute-start | bytes 122888 | tf_op jit(solution)/shard_map/ppermute | solution.py:26
  118.5 13.0 %collective-permute-start.7 = (f32[5,4,16,32]{3,2,1,0:T(8,128)S(1)}, f32[5,4,16,32]{3,2,1,0:T(8,128)S(1)}, u32[]{:S(2)}, u32[]{:S(2)}) collective-permute-start(f32[5,4,16,32]{3,2,1,0:T(8,128)S(1)} %copy.40), channel_id=1, source_target_pairs={{8,0},{12,4},{16,8},{20,12},{24,16},{28,20},{9,1},{13,5},{17,9},{2... | collective-permute-start | bytes 122888 | tf_op jit(solution)/shard_map/ppermute | solution.py:26
  119.8 11.6 %collective-permute-start.6 = (f32[5,4,16,32]{3,2,1,0:T(8,128)S(1)}, f32[5,4,16,32]{3,2,1,0:T(8,128)S(1)}, u32[]{:S(2)}, u32[]{:S(2)}) collective-permute-start(f32[5,4,16,32]{3,2,1,0:T(8,128)S(1)} %copy.40), channel_id=1, source_target_pairs={{4,0},{8,4},{12,8},{16,12},{20,16},{24,20},{28,24},{5,1},{9,5},{13... | collective-permute-start | bytes 122888 | tf_op jit(solution)/shard_map/ppermute | solution.py:26
  121.1 10.3 %collective-permute-start.5 = (f32[5,4,16,32]{3,2,1,0:T(8,128)S(1)}, f32[5,4,16,32]{3,2,1,0:T(8,128)S(1)}, u32[]{:S(2)}, u32[]{:S(2)}) collective-permute-start(f32[5,4,16,32]{3,2,1,0:T(8,128)S(1)} %copy.40), channel_id=1, source_target_pairs={{0,4},{4,8},{8,12},{12,16},{16,20},{20,24},{24,28},{1,5},{5,9},{9,... | collective-permute-start | bytes 122888 | tf_op jit(solution)/shard_map/ppermute | solution.py:26
  135.8 5.4 %collective-permute-start.8 = (f32[2,5,8,64]{3,2,1,0:T(8,128)S(1)}, f32[2,5,8,64]{3,2,1,0:T(8,128)S(1)}, u32[]{:S(2)}, u32[]{:S(2)}) collective-permute-start(f32[2,5,8,64]{3,2,1,0:T(8,128)S(1)} %get-tuple-element.135), channel_id=1, source_target_pairs={{0,4},{4,8},{8,12},{12,16},{16,20},{20,24},{24,28},{1,5},{5,9},{9,... | collective-permute-start | bytes 61448 | tf_op jit(solution)/shard_map/ppermute | solution.py:26
  140.0 4.7 %collective-permute-start.9 = (f32[2,5,8,64]{3,2,1,0:T(8,128)S(1)}, f32[2,5,8,64]{3,2,1,0:T(8,128)S(1)}, u32[]{:S(2)}, u32[]{:S(2)}) collective-permute-start(f32[2,5,8,64]{3,2,1,0:T(8,128)S(1)} %get-tuple-element.136), channel_id=1, source_target_pairs={{4,0},{8,4},{12,8},{16,12},{20,16},{24,20},{28,24},{5,1},{9,5},{13... | collective-permute-start | bytes 61448 | tf_op jit(solution)/shard_map/ppermute | solution.py:26
  144.7 7.7 %collective-permute-start.10 = (f32[2,18,5,64]{3,2,1,0:T(8,128)S(1)}, f32[2,18,5,64]{3,2,1,0:T(8,128)S(1)}, u32[]{:S(2)}, u32[]{:S(2)}) collective-permute-start(f32[2,18,5,64]{3,2,1,0:T(8,128)S(1)} %get-tuple-element.91), channel_id=1, source_target_pairs={{0,1},{1,2},{2,3},{4,5},{5,6},{6,7},{8,9},{9,10},{10,11},{12,13},{... | collective-permute-start | bytes 138248 | tf_op jit(solution)/shard_map/ppermute | solution.py:26
  150.4 6.5 %collective-permute-start.11 = (f32[2,18,5,64]{3,2,1,0:T(8,128)S(1)}, f32[2,18,5,64]{3,2,1,0:T(8,128)S(1)}, u32[]{:S(2)}, u32[]{:S(2)}) collective-permute-start(f32[2,18,5,64]{3,2,1,0:T(8,128)S(1)} %get-tuple-element.92), channel_id=1, source_target_pairs={{1,0},{2,1},{3,2},{5,4},{6,5},{7,6},{9,8},{10,9},{11,10},{13,12},{... | collective-permute-start | bytes 138248 | tf_op jit(solution)/shard_map/ppermute | solution.py:26
  157.5 0.7 copy-start.10
  158.6 1.1 copy-start.1
  158.6 1.3 copy-start.6
where the time goes:
time: 163 us; the launch traced here: 162 us
  other arithmetic  64.4 us (40%)
  starting transfers between devices  36.6 us (22%)
  waiting for transfers between devices  35 us (21%)
  local copies, waits for them, and re-layouts  16.8 us (10%)
  blocking collectives  4.37 us (3%)
  matrix products  4.22 us (3%)
    ppermute x12, starting transfers between devices, shift_from(): return lax.ppermute(cells, axis, pairs)  36.6 us
    ppermute x12, waiting for transfers between devices, shift_from(): return lax.ppermute(cells, axis, pairs)  35 us
    select_n x2, other arithmetic, local(): kx = jnp.where(inside, lookup(ids, soil_table, 0), 0.0)  11.7 us
    select_n x2, other arithmetic, local(): kz = jnp.where(inside, lookup(ids, soil_table, 2), 0.0)  11.4 us
    select_n x1, other arithmetic, local(): store = jnp.where(inside, store, 0.0)  11 us
    select_n x2, other arithmetic, local(): ky = jnp.where(inside, lookup(ids, soil_table, 1), 0.0)  11 us
    all_gather x1, blocking collectives, local(): cpack = lax.all_gather(cpack, 'gy', axis=2, tiled=True)  4.37 us
    add x7, other arithmetic, chebyshev(): iterate = win(iterate, n, cur, nxt) + update  3.87 us
  transfers between devices with their start and end apart: 12, of which 7 were waited for; matrix products, arithmetic and copies ran while one was open for 2% of the time, Pallas kernels for 0%

commit v1 on v0

--- a/solution.py
+++ b/solution.py
@@ -192,7 +192,14 @@
     nc = b2.shape[0]
     reach = 2
     cpack = jnp.concatenate([b2[None], coarse_own], axis=0)
-    cpack = lax.all_gather(cpack, "gy", axis=2, tiled=True)
+    peers = lax.axis_size("gy")
+    hops = [(i_2, (i_2 + 1) % peers) for i_2 in range(peers)]
+    pieces = [cpack]
+    for far in range(1, peers):
+        pieces = [lax.ppermute(pieces[0], "gy", hops), *pieces]
+    result = jnp.concatenate(pieces, axis=2)
+    shift = (lax.axis_index("gy") + 1) * pieces[-1].shape[2]
+    cpack = jnp.roll(result, shift, axis=2)
     parts = [shift_from(cpack, "gx", -d) for d in range(reach, 0, -1)]
     parts += [cpack]
     parts += [shift_from(cpack, "gx", d) for d in range(1, reach + 1)]

time: 163 us -> 179 us (1.098); the launches traced: 162 us -> 176 us
  local copies, waits for them, and re-layouts: 16.8 us -> 27.4 us
  blocking collectives: 4.37 us -> 0 us
  waiting for transfers between devices: 35 us -> 38.8 us
  starting transfers between devices: 36.6 us -> 39.5 us
    concatenate x1, local copies, waits for them, and re-layouts: 0.01 us -> 5.9 us  [local(): cpack = jnp.roll(result, shift, axis=2)]
    ppermute x0 -> x3, starting transfers between devices: none -> 4.64 us  [local(): pieces = [lax.ppermute(pieces[0], 'gy', hops), *pieces]]
    all_gather x1 -> x0, blocking collectives: 4.37 us -> none  [local(): cpack = lax.all_gather(cpack, 'gy', axis=2, tiled=True)]
    ppermute x0 -> x3, waiting for transfers between devices: none -> 3.73 us  [local(): pieces = [lax.ppermute(pieces[0], 'gy', hops), *pieces]]
    unnamed x29 -> x50, local copies, waits for them, and re-layouts: 0.66 us -> 2.96 us
  transfers between devices with their start and end apart: 12 -> 15, of which waited for: 7 -> 10; matrix products, arithmetic and copies ran while one was open for 2% -> 3% of each run, Pallas kernels for 0% -> 0%
where the time goes in v1:
time: 179 us; the launch traced here: 176 us
  other arithmetic  65.7 us (37%)
  starting transfers between devices  39.5 us (22%)
  waiting for transfers between devices  38.8 us (22%)
  local copies, waits for them, and re-layouts  27.4 us (15%)
  matrix products  3.56 us (2%)
    ppermute x12, waiting for transfers between devices, shift_from(): return lax.ppermute(cells, axis, pairs)  35.1 us
    ppermute x12, starting transfers between devices, shift_from(): return lax.ppermute(cells, axis, pairs)  34.9 us
    select_n x2, other arithmetic, local(): kx = jnp.where(inside, lookup(ids, soil_table, 0), 0.0)  11.7 us
    select_n x2, other arithmetic, local(): ky = jnp.where(inside, lookup(ids, soil_table, 1), 0.0)  11.2 us
    select_n x1, other arithmetic, local(): store = jnp.where(inside, store, 0.0)  11.2 us
    select_n x2, other arithmetic, local(): kz = jnp.where(inside, lookup(ids, soil_table, 2), 0.0)  10.9 us
    concatenate x1, local copies, waits for them, and re-layouts, local(): cpack = jnp.roll(result, shift, axis=2)  5.9 us
    ppermute x3, starting transfers between devices, local(): pieces = [lax.ppermute(pieces[0], 'gy', hops), *pieces]  4.64 us
  transfers between devices with their start and end apart: 15, of which 10 were waited for; matrix products, arithmetic and copies ran while one was open for 3% of the time, Pallas kernels for 0%

profile of v1, /device:TPU:1, one launch (start us, length us, event | category | flops | bytes accessed | tf_op | source)
XLA Modules:
  0.0 176.1 jit_solution(12937632107012172874)
XLA Ops:
  0.0 1.0 fusion.164
  1.0 1.1 copy_bitcast_fusion
  2.1 4.0 %collective-permute-start = (f32[3,10,16,128]{3,1,2,0:T(8,128)S(1)}, f32[3,10,16,128]{3,1,2,0:T(8,128)S(1)}, u32[]{:S(2)}, u32[]{:S(2)}) collective-permute-start(f32[3,10,16,128]{3,1,2,0:T(8,128)S(1)} %get-tuple-element.62), channel_id=1, source_target_pairs={{0,4},{4,8},{8,12},{12,16},{16,20},{20,24},{24,28},{1,5},{5,9},{9,... | collective-permute-start | bytes 737288 | tf_op jit(solution)/shard_map/ppermute | solution.py:26
  6.1 1.3 collective-permute-start.1
  8.0 0.6 and_select_fusion.4
  8.6 0.7 fusion.465
  9.2 13.1 %collective-permute-done = f32[3,10,16,128]{3,1,2,0:T(8,128)S(1)} collective-permute-done((f32[3,10,16,128]{3,1,2,0:T(8,128)S(1)}, f32[3,10,16,128]{3,1,2,0:T(8,128)S(1)}, u32[]{:S(2)}, u32[]{:S(2)}) %collective-permute-start) | collective-permute-done | bytes 245792 | tf_op jit(solution)/shard_map/ppermute | solution.py:26
  22.5 4.6 %collective-permute-start.2 = (f32[3,36,10,128]{3,1,2,0:T(8,128)S(1)}, f32[3,36,10,128]{3,1,2,0:T(8,128)S(1)}, u32[]{:S(2)}, u32[]{:S(2)}) collective-permute-start(f32[3,36,10,128]{3,1,2,0:T(8,128)S(1)} %get-tuple-element.37), channel_id=1, source_target_pairs={{0,1},{1,2},{2,3},{4,5},{5,6},{6,7},{8,9},{9,10},{10,11},{12,13},{... | collective-permute-start | bytes 1658888 | tf_op jit(solution)/shard_map/ppermute | solution.py:26
  27.1 1.9 %collective-permute-start.3 = (f32[3,36,10,128]{3,1,2,0:T(8,128)S(1)}, f32[3,36,10,128]{3,1,2,0:T(8,128)S(1)}, u32[]{:S(2)}, u32[]{:S(2)}) collective-permute-start(f32[3,36,10,128]{3,1,2,0:T(8,128)S(1)} %get-tuple-element.38), channel_id=1, source_target_pairs={{1,0},{2,1},{3,2},{5,4},{6,5},{7,6},{9,8},{10,9},{11,10},{13,12},{... | collective-permute-start | bytes 1658888 | tf_op jit(solution)/shard_map/ppermute | solution.py:26
  29.0 0.7 fusion.464
  29.7 0.7 fusion.463
  30.6 3.6 %collective-permute-done.2 = f32[3,36,10,128]{3,1,2,0:T(8,128)S(1)} collective-permute-done((f32[3,36,10,128]{3,1,2,0:T(8,128)S(1)}, f32[3,36,10,128]{3,1,2,0:T(8,128)S(1)}, u32[]{:S(2)}, u32[]{:S(2)}) %collective-permute-start.2) | collective-permute-done | bytes 552992 | tf_op jit(solution)/shard_map/ppermute | solution.py:26
  34.1 4.4 %collective-permute-done.3 = f32[3,36,10,128]{3,1,2,0:T(8,128)S(1)} collective-permute-done((f32[3,36,10,128]{3,1,2,0:T(8,128)S(1)}, f32[3,36,10,128]{3,1,2,0:T(8,128)S(1)}, u32[]{:S(2)}, u32[]{:S(2)}) %collective-permute-start.3) | collective-permute-done | bytes 552992 | tf_op jit(solution)/shard_map/ppermute | solution.py:26
  38.7 6.1 %broadcast_select_fusion.3 = (f32[1,36,36,128]{3,1,2,0:T(8,128)S(1)}, pred[1,36,36,128]{3,1,2,0:T(8,128)(4,1)S(1)}, pred[1,36,36,128]{3,1,2,0:T(8,128)(4,1)S(1)}...) fusion(pred[36,36]{0,1:T(8,128)(4,1)S(1)} %broadcast_and_fusion, ...), kind=kLoop, calls=%fused_computation.137 | loop fusion | flops 2654208 | bytes 3816752 | tf_op jit(solution)/shard_map/jit(_where)/select_n | solution.py:169
  44.8 5.6 %broadcast_select_fusion.2 = f32[1,36,36,128]{3,1,2,0:T(8,128)S(1)} fusion(pred[36,36]{0,1:T(8,128)(4,1)S(1)} %broadcast_and_fusion, pred[1,36,36,128]{3,1,2,0:T(8,128)(4,1)S(1)} %get-tuple-element.33, pred[1,36,36,128]{3,1,2,0:T(8,128)(4,1)S(1)} %get-tuple-element.32, pred[1,36,36,128]{3,1,2,0:T(8,128)(4,1)S(1)} %get-tuple-element.31, ...), kind=kLoop, calls=%fused_computation.136 | loop fusion | flops 1327104 | bytes 1826096 | tf_op jit(solution)/shard_map/jit(_where)/select_n | solution.py:170
  50.5 5.6 %bitcast_select_fusion.2 = f32[36,36,128]{2,0,1:T(8,128)S(1)} fusion(pred[36,36]{0,1:T(8,128)(4,1)S(1)} %broadcast_and_fusion, pred[1,36,36,128]{3,1,2,0:T(8,128)(4,1)S(1)} %get-tuple-element.33, pred[1,36,36,128]{3,1,2,0:T(8,128)(4,1)S(1)} %get-tuple-element.32, pred[1,36,36,128]{3,1,2,0:T(8,128)(4,1)S(1)} %get-tuple-element.31, ...), kind=kLoop, calls=%fused_computation.31 | loop fusion | flops 1327104 | bytes 1826096 | tf_op jit(solution)/shard_map/jit(_where)/select_n | solution.py:170
  56.1 5.4 %broadcast_select_fusion.1 = f32[1,36,36,128]{3,1,2,0:T(8,128)S(1)} fusion(pred[36,36]{0,1:T(8,128)(4,1)S(1)} %broadcast_and_fusion, pred[1,36,36,128]{3,1,2,0:T(8,128)(4,1)S(1)} %get-tuple-element.33, pred[1,36,36,128]{3,1,2,0:T(8,128)(4,1)S(1)} %get-tuple-element.32, pred[1,36,36,128]{3,1,2,0:T(8,128)(4,1)S(1)} %get-tuple-element.31, ...), kind=kLoop, calls=%fused_computation.135 | loop fusion | flops 1327104 | bytes 1826096 | tf_op jit(solution)/shard_map/jit(_where)/select_n | solution.py:171
  61.6 5.4 %bitcast_select_fusion.1 = f32[36,36,128]{2,0,1:T(8,128)S(1)} fusion(pred[36,36]{0,1:T(8,128)(4,1)S(1)} %broadcast_and_fusion, pred[1,36,36,128]{3,1,2,0:T(8,128)(4,1)S(1)} %get-tuple-element.33, pred[1,36,36,128]{3,1,2,0:T(8,128)(4,1)S(1)} %get-tuple-element.32, pred[1,36,36,128]{3,1,2,0:T(8,128)(4,1)S(1)} %get-tuple-element.31, ...), kind=kLoop, calls=%fused_computation.30 | loop fusion | flops 1327104 | bytes 1826096 | tf_op jit(solution)/shard_map/jit(_where)/select_n | solution.py:171
  67.0 0.7 copy.21
  67.7 11.2 %broadcast_select_fusion = (f32[1,36,36,128]{3,1,2,0:T(8,128)S(1)}, f32[1,36,36,128]{3,1,2,0:T(8,128)S(1)}) fusion(pred[36,36]{0,1:T(8,128)(4,1)S(1)} %broadcast_and_fusion, f32[3,36,36,128]{3,1,2,0:T(8,128)S(1)} %pad_maximum_fusion.1, pred[1,36,36,128]{3,1,2,0:T(8,128)(4,1)S(1)} %get-tuple-element.33, pred[1,36,36,128]{3,1,2,0:T(8,128)(4,1)S(1)} %get-tuple-element.32, ...), kind=kLoop, calls=%fused_computation.134 | loop fusion | flops 3317760 | bytes 3153232 | tf_op jit(solution)/shard_map/jit(_where)/select_n | solution.py:175
  78.9 0.7 copy.24
  79.6 0.7 copy.22
  80.3 0.7 copy.23
  81.0 2.7 %pad_maximum_fusion = f32[4,18,2,36,128]{4,0,3,2,1:T(4,128)S(1)} fusion(f32[1,18,2,36,128]{4,0,3,2,1:T(1,128)S(1)} %bitcast.252, f32[1,18,2,36,128]{4,0,3,2,1:T(1,128)S(1)} %bitcast.254, f32[1,18,2,36,128]{4,0,3,2,1:T(1,128)S(1)} %bitcast.253, f32[1,18,2,36,128]{4,0,3,2,1:T(1,128)S(1)} %bitcast.251), kind=kLoop, calls=%fused_computation | loop fusion | flops 1990656 | bytes 5308416 | tf_op jit(solution)/shard_map/stack | solution.py:176
  84.1 0.8 fusion
  84.9 0.7 fusion.3
  85.6 0.7 slice.2155
  86.3 0.8 multiply_bitcast_fusion
  87.0 0.7 slice_bitcast_fusion.4
  87.9 5.6 %bitcast_select_fusion.3 = (f32[36,36,128]{2,0,1:T(8,128)S(1)}, f32[36,36,128]{2,0,1:T(8,128)S(1)}) fusion(pred[36,36]{0,1:T(8,128)(4,1)S(1)} %broadcast_and_fusion, pred[1,36,36,128]{3,1,2,0:T(8,128)(4,1)S(1)} %get-tuple-element.33, pred[1,36,36,128]{3,1,2,0:T(8,128)(4,1)S(1)} %get-tuple-element.32, pred[1,36,36,128]{3,1,2,0:T(8,128)(4,1)S(1)} %get-tuple-element.31, ...), kind=kLoop, calls=%fused_computation.32 | loop fusion | flops 1492992 | bytes 3153200 | tf_op jit(solution)/shard_map/jit(_where)/select_n | solution.py:169
  94.0 0.7 fusion.15
  95.2 1.2 slice_add_fusion.5
  96.9 1.2 fusion.33
  98.4 0.8 divide_multiply_fusion
  99.3 0.7 divide_multiply_fusion.1
  100.0 1.7 fusion.58
  101.7 2.0 %reshape.377 = f32[14,2,28,128]{3,1,0,2:T(2,128)} reshape(f32[28,28,128]{2,0,1:T(8,128)} %fusion.58) | data formatting | bytes 802816 | tf_op jit(solution)/shard_map/reshape | solution.py:59
  103.7 1.5 fusion.427
  105.6 1.5 add_maximum_fusion.1
  108.6 0.6 fusion.339
  109.7 0.6 copy-done.14
  110.3 1.2 collective-permute-done.4
  111.5 0.6 copy-done.16
  112.1 2.2 %collective-permute-start.5 = (f32[5,4,4,32]{3,2,1,0:T(4,128)S(1)}, f32[5,4,4,32]{3,2,1,0:T(4,128)}, u32[]{:S(2)}, u32[]{:S(2)}) collective-permute-start(f32[5,4,4,32]{3,2,1,0:T(4,128)S(1)} %collective-permute-done.4), channel_id=1, source_target_pairs={{0,1},{1,2},{2,3},{3,0},{4,5},{5,6},{6,7},{7,4},{8,9},{9,10},{10,1... | collective-permute-start | bytes 30728 | tf_op jit(solution)/shard_map/ppermute | solution.py:199
  114.4 1.1 collective-permute-done.5
  115.5 2.4 %collective-permute-start.6 = (f32[5,4,4,32]{3,2,1,0:T(4,128)}, f32[5,4,4,32]{3,2,1,0:T(4,128)}, u32[]{:S(2)}, u32[]{:S(2)}) collective-permute-start(f32[5,4,4,32]{3,2,1,0:T(4,128)} %collective-permute-done.5), channel_id=1, source_target_pairs={{0,1},{1,2},{2,3},{3,0},{4,5},{5,6},{6,7},{7,4},{8,9},{9,10},{10,1... | collective-permute-start | bytes 30728 | tf_op jit(solution)/shard_map/ppermute | solution.py:199
  117.9 1.4 collective-permute-done.6
  119.3 5.9 %concatenate.188 = f32[5,4,32,32]{3,2,1,0:T(8,128)} concatenate(f32[5,4,4,32]{3,2,1,0:T(4,128)} %collective-permute-done.6, f32[5,4,4,32]{3,2,1,0:T(4,128)} %collective-permute-done.5, f32[5,4,4,32]{3,2,1,0:T(4,128)} %copy-done.16, f32[5,4,4,32]{3,2,1,0:T(4,128)} %copy-done.14, f32[5,4,4,32]{3,2,1,0:T(4,128)} %collective-permute-done.6, f32[5,4,4,32]{3,2,1,0:T(4,128)} %collective-permute-done.5, ...), dimensions={2} | concatenate | bytes 163840 | tf_op jit(solution)/shard_map/jit(_roll_dynamic)/concatenate | solution.py:202
  125.2 1.0 constant_dynamic-slice_fusion
  126.2 5.1 %collective-permute-start.7 = (f32[5,4,16,32]{3,2,1,0:T(8,128)S(1)}, f32[5,4,16,32]{3,2,1,0:T(8,128)S(1)}, u32[]{:S(2)}, u32[]{:S(2)}) collective-permute-start(f32[5,4,16,32]{3,2,1,0:T(8,128)S(1)} %constant_dynamic-slice_fusion), channel_id=1, source_target_pairs={{0,8},{4,12},{8,16},{12,20},{16,24},{20,28},{1,9},{5,13},{9,17},{1... | collective-permute-start | bytes 122888 | tf_op jit(solution)/shard_map/ppermute | solution.py:26
  131.2 0.8 dynamic-slice_bitcast_fusion
  132.1 1.3 collective-permute-start.10
  133.4 1.3 collective-permute-start.9
  134.7 4.2 %collective-permute-start.8 = (f32[5,4,16,32]{3,2,1,0:T(8,128)S(1)}, f32[5,4,16,32]{3,2,1,0:T(8,128)S(1)}, u32[]{:S(2)}, u32[]{:S(2)}) collective-permute-start(f32[5,4,16,32]{3,2,1,0:T(8,128)S(1)} %constant_dynamic-slice_fusion), channel_id=1, source_target_pairs={{0,4},{4,8},{8,12},{12,16},{16,20},{20,24},{24,28},{1,5},{5,9},{9,... | collective-permute-start | bytes 122888 | tf_op jit(solution)/shard_map/ppermute | solution.py:26
  138.9 6.1 %collective-permute-done.8 = f32[5,4,16,32]{3,2,1,0:T(8,128)S(1)} collective-permute-done((f32[5,4,16,32]{3,2,1,0:T(8,128)S(1)}, f32[5,4,16,32]{3,2,1,0:T(8,128)S(1)}, u32[]{:S(2)}, u32[]{:S(2)}) %collective-permute-start.8) | collective-permute-done | bytes 40992 | tf_op jit(solution)/shard_map/ppermute | solution.py:26
  145.0 1.0 constant_dynamic-update-slice_fusion.2
  150.4 0.9 bitcast_add_fusion
  151.2 4.1 %collective-permute-start.11 = (f32[2,5,8,64]{3,2,1,0:T(8,128)S(1)}, f32[2,5,8,64]{3,2,1,0:T(8,128)S(1)}, u32[]{:S(2)}, u32[]{:S(2)}) collective-permute-start(f32[2,5,8,64]{3,2,1,0:T(8,128)S(1)} %get-tuple-element.129), channel_id=1, source_target_pairs={{0,4},{4,8},{8,12},{12,16},{16,20},{20,24},{24,28},{1,5},{5,9},{9,... | collective-permute-start | bytes 61448 | tf_op jit(solution)/shard_map/ppermute | solution.py:26
  155.3 1.3 collective-permute-start.12
  156.7 3.4 %collective-permute-done.12 = f32[2,5,8,64]{3,2,1,0:T(8,128)S(1)} collective-permute-done((f32[2,5,8,64]{3,2,1,0:T(8,128)S(1)}, f32[2,5,8,64]{3,2,1,0:T(8,128)S(1)}, u32[]{:S(2)}, u32[]{:S(2)}) %collective-permute-start.12) | collective-permute-done | bytes 20512 | tf_op jit(solution)/shard_map/ppermute | solution.py:26
  160.1 3.9 %collective-permute-start.13 = (f32[2,18,5,64]{3,2,1,0:T(8,128)S(1)}, f32[2,18,5,64]{3,2,1,0:T(8,128)S(1)}, u32[]{:S(2)}, u32[]{:S(2)}) collective-permute-start(f32[2,18,5,64]{3,2,1,0:T(8,128)S(1)} %get-tuple-element.85), channel_id=1, source_target_pairs={{0,1},{1,2},{2,3},{4,5},{5,6},{6,7},{8,9},{9,10},{10,11},{12,13},{... | collective-permute-start | bytes 138248 | tf_op jit(solution)/shard_map/ppermute | solution.py:26
  164.1 1.9 %collective-permute-start.14 = (f32[2,18,5,64]{3,2,1,0:T(8,128)S(1)}, f32[2,18,5,64]{3,2,1,0:T(8,128)S(1)}, u32[]{:S(2)}, u32[]{:S(2)}) collective-permute-start(f32[2,18,5,64]{3,2,1,0:T(8,128)S(1)} %get-tuple-element.86), channel_id=1, source_target_pairs={{1,0},{2,1},{3,2},{5,4},{6,5},{7,6},{9,8},{10,9},{11,10},{13,12},{... | collective-permute-start | bytes 138248 | tf_op jit(solution)/shard_map/ppermute | solution.py:26
  166.2 4.4 %collective-permute-done.14 = f32[2,18,5,64]{3,2,1,0:T(8,128)S(1)} collective-permute-done((f32[2,18,5,64]{3,2,1,0:T(8,128)S(1)}, f32[2,18,5,64]{3,2,1,0:T(8,128)S(1)}, u32[]{:S(2)}, u32[]{:S(2)}) %collective-permute-start.14) | collective-permute-done | bytes 46112 | tf_op jit(solution)/shard_map/ppermute | solution.py:26
  175.4 0.7 copy.31
  (161 shorter events, 14.4 us)
Async XLA Ops:
  0.0 8.6 %copy-start.17 = (f32[5,8]{1,0:T(8,128)S(1)}, f32[5,8]{1,0:T(8,128)}, u32[]{:S(2)}) copy-start(f32[5,8]{1,0:T(8,128)} %param.7) | copy-start | bytes 484
  2.1 20.2 %collective-permute-start = (f32[3,10,16,128]{3,1,2,0:T(8,128)S(1)}, f32[3,10,16,128]{3,1,2,0:T(8,128)S(1)}, u32[]{:S(2)}, u32[]{:S(2)}) collective-permute-start(f32[3,10,16,128]{3,1,2,0:T(8,128)S(1)} %get-tuple-element.62), channel_id=1, source_target_pairs={{0,4},{4,8},{8,12},{12,16},{16,20},{20,24},{24,28},{1,5},{5,9},{9,... | collective-permute-start | bytes 737288 | tf_op jit(solution)/shard_map/ppermute | solution.py:26
  6.1 16.2 %collective-permute-start.1 = (f32[3,10,16,128]{3,1,2,0:T(8,128)S(1)}, f32[3,10,16,128]{3,1,2,0:T(8,128)S(1)}, u32[]{:S(2)}, u32[]{:S(2)}) collective-permute-start(f32[3,10,16,128]{3,1,2,0:T(8,128)S(1)} %get-tuple-element.63), channel_id=1, source_target_pairs={{4,0},{8,4},{12,8},{16,12},{20,16},{24,20},{28,24},{5,1},{9,5},{13... | collective-permute-start | bytes 737288 | tf_op jit(solution)/shard_map/ppermute | solution.py:26
  7.4 97.9 %copy-start.18 = (s32[128]{0:T(128)}, s32[128]{0:T(128)S(1)}, u32[]{:S(2)}) copy-start(s32[128]{0:T(128)S(1)} %and_select_fusion.3) | copy-start | bytes 1540
  22.5 11.6 %collective-permute-start.2 = (f32[3,36,10,128]{3,1,2,0:T(8,128)S(1)}, f32[3,36,10,128]{3,1,2,0:T(8,128)S(1)}, u32[]{:S(2)}, u32[]{:S(2)}) collective-permute-start(f32[3,36,10,128]{3,1,2,0:T(8,128)S(1)} %get-tuple-element.37), channel_id=1, source_target_pairs={{0,1},{1,2},{2,3},{4,5},{5,6},{6,7},{8,9},{9,10},{10,11},{12,13},{... | collective-permute-start | bytes 1658888 | tf_op jit(solution)/shard_map/ppermute | solution.py:26
  27.1 11.5 %collective-permute-start.3 = (f32[3,36,10,128]{3,1,2,0:T(8,128)S(1)}, f32[3,36,10,128]{3,1,2,0:T(8,128)S(1)}, u32[]{:S(2)}, u32[]{:S(2)}) collective-permute-start(f32[3,36,10,128]{3,1,2,0:T(8,128)S(1)} %get-tuple-element.38), channel_id=1, source_target_pairs={{1,0},{2,1},{3,2},{5,4},{6,5},{7,6},{9,8},{10,9},{11,10},{13,12},{... | collective-permute-start | bytes 1658888 | tf_op jit(solution)/shard_map/ppermute | solution.py:26
  93.5 6.5 %copy-start = (f32[36,36,128]{2,0,1:T(8,128)}, f32[36,36,128]{2,0,1:T(8,128)S(1)}, u32[]{:S(2)}) copy-start(f32[36,36,128]{2,0,1:T(8,128)S(1)} %get-tuple-element.145) | copy-start | bytes 1990660
  94.8 2.1 %copy-start.8 = (f32[34,34,128]{2,0,1:T(8,128)}, f32[34,34,128]{2,0,1:T(8,128)S(1)}, u32[]{:S(2)}) copy-start(f32[34,34,128]{2,0,1:T(8,128)S(1)} %get-tuple-element.25) | copy-start | bytes 1775620
  103.7 3.3 %copy-start.22 = (s32[28]{0:T(128)S(1)}, s32[28]{0:T(128)}, u32[]{:S(2)}) copy-start(s32[28]{0:T(128)} %and_select_fusion.4) | copy-start | bytes 340
  103.7 3.7 %copy-start.2 = (f32[18,18,63]{2,1,0:T(8,128)S(1)}, f32[18,18,63]{2,1,0:T(8,128)}, u32[]{:S(2)}) copy-start(f32[18,18,63]{2,1,0:T(8,128)} %divide_multiply_fusion) | copy-start | bytes 244948
  103.7 3.8 %copy-start.4 = (f32[17,18,64]{2,1,0:T(8,128)S(1)}, f32[17,18,64]{2,1,0:T(8,128)}, u32[]{:S(2)}) copy-start(f32[17,18,64]{2,1,0:T(8,128)} %multiply_bitcast_fusion) | copy-start | bytes 235012
  103.7 3.8 %copy-start.6 = (f32[18,17,64]{2,1,0:T(8,128)S(1)}, f32[18,17,64]{2,1,0:T(8,128)}, u32[]{:S(2)}) copy-start(f32[18,17,64]{2,1,0:T(8,128)} %divide_multiply_fusion.1) | copy-start | bytes 235012
  103.7 3.8 %copy-start.10 = (f32[18,18,64]{2,1,0:T(8,128)S(1)}, f32[18,18,64]{2,1,0:T(8,128)}, u32[]{:S(2)}) copy-start(f32[18,18,64]{2,1,0:T(8,128)} %get-tuple-element.40) | copy-start | bytes 248836
  107.5 0.9 copy-start.15
  107.5 0.9 copy-start.20
  108.2 1.1 copy-start.12
  109.7 0.6 copy-start.14
  110.3 1.2 collective-permute-start.4
  111.5 0.6 copy-start.16
  112.1 3.3 %collective-permute-start.5 = (f32[5,4,4,32]{3,2,1,0:T(4,128)S(1)}, f32[5,4,4,32]{3,2,1,0:T(4,128)}, u32[]{:S(2)}, u32[]{:S(2)}) collective-permute-start(f32[5,4,4,32]{3,2,1,0:T(4,128)S(1)} %collective-permute-done.4), channel_id=1, source_target_pairs={{0,1},{1,2},{2,3},{3,0},{4,5},{5,6},{6,7},{7,4},{8,9},{9,10},{10,1... | collective-permute-start | bytes 30728 | tf_op jit(solution)/shard_map/ppermute | solution.py:199
  115.5 3.8 %collective-permute-start.6 = (f32[5,4,4,32]{3,2,1,0:T(4,128)}, f32[5,4,4,32]{3,2,1,0:T(4,128)}, u32[]{:S(2)}, u32[]{:S(2)}) collective-permute-start(f32[5,4,4,32]{3,2,1,0:T(4,128)} %collective-permute-done.5), channel_id=1, source_target_pairs={{0,1},{1,2},{2,3},{3,0},{4,5},{5,6},{6,7},{7,4},{8,9},{9,10},{10,1... | collective-permute-start | bytes 30728 | tf_op jit(solution)/shard_map/ppermute | solution.py:199
  126.2 12.7 %collective-permute-start.7 = (f32[5,4,16,32]{3,2,1,0:T(8,128)S(1)}, f32[5,4,16,32]{3,2,1,0:T(8,128)S(1)}, u32[]{:S(2)}, u32[]{:S(2)}) collective-permute-start(f32[5,4,16,32]{3,2,1,0:T(8,128)S(1)} %constant_dynamic-slice_fusion), channel_id=1, source_target_pairs={{0,8},{4,12},{8,16},{12,20},{16,24},{20,28},{1,9},{5,13},{9,17},{1... | collective-permute-start | bytes 122888 | tf_op jit(solution)/shard_map/ppermute | solution.py:26
  132.1 14.0 %collective-permute-start.10 = (f32[5,4,16,32]{3,2,1,0:T(8,128)S(1)}, f32[5,4,16,32]{3,2,1,0:T(8,128)S(1)}, u32[]{:S(2)}, u32[]{:S(2)}) collective-permute-start(f32[5,4,16,32]{3,2,1,0:T(8,128)S(1)} %constant_dynamic-slice_fusion), channel_id=1, source_target_pairs={{8,0},{12,4},{16,8},{20,12},{24,16},{28,20},{9,1},{13,5},{17,9},{2... | collective-permute-start | bytes 122888 | tf_op jit(solution)/shard_map/ppermute | solution.py:26
  133.4 12.6 %collective-permute-start.9 = (f32[5,4,16,32]{3,2,1,0:T(8,128)S(1)}, f32[5,4,16,32]{3,2,1,0:T(8,128)S(1)}, u32[]{:S(2)}, u32[]{:S(2)}) collective-permute-start(f32[5,4,16,32]{3,2,1,0:T(8,128)S(1)} %constant_dynamic-slice_fusion), channel_id=1, source_target_pairs={{4,0},{8,4},{12,8},{16,12},{20,16},{24,20},{28,24},{5,1},{9,5},{13... | collective-permute-start | bytes 122888 | tf_op jit(solution)/shard_map/ppermute | solution.py:26
  134.7 10.3 %collective-permute-start.8 = (f32[5,4,16,32]{3,2,1,0:T(8,128)S(1)}, f32[5,4,16,32]{3,2,1,0:T(8,128)S(1)}, u32[]{:S(2)}, u32[]{:S(2)}) collective-permute-start(f32[5,4,16,32]{3,2,1,0:T(8,128)S(1)} %constant_dynamic-slice_fusion), channel_id=1, source_target_pairs={{0,4},{4,8},{8,12},{12,16},{16,20},{20,24},{24,28},{1,5},{5,9},{9,... | collective-permute-start | bytes 122888 | tf_op jit(solution)/shard_map/ppermute | solution.py:26
  149.2 0.7 copy-start.21
  149.3 2.0 %copy-start.13 = (f32[1,8,8,64]{3,2,1,0:T(8,128)S(1)}, f32[1,8,8,64]{3,2,1,0:T(8,128)}, u32[]{:S(2)}) copy-start(f32[1,8,8,64]{3,2,1,0:T(8,128)} %get-tuple-element.108) | copy-start | bytes 49156
  149.8 21.0 %copy-start.3 = (f32[18,18,63]{2,1,0:T(8,128)S(1)}, f32[18,18,63]{2,1,0:T(8,128)}, u32[]{:S(2)}) copy-start(f32[18,18,63]{2,1,0:T(8,128)} %divide_multiply_fusion) | copy-start | bytes 244948
  149.8 21.1 %copy-start.5 = (f32[17,18,64]{2,1,0:T(8,128)S(1)}, f32[17,18,64]{2,1,0:T(8,128)}, u32[]{:S(2)}) copy-start(f32[17,18,64]{2,1,0:T(8,128)} %multiply_bitcast_fusion) | copy-start | bytes 235012
  149.9 21.1 %copy-start.7 = (f32[18,17,64]{2,1,0:T(8,128)S(1)}, f32[18,17,64]{2,1,0:T(8,128)}, u32[]{:S(2)}) copy-start(f32[18,17,64]{2,1,0:T(8,128)} %divide_multiply_fusion.1) | copy-start | bytes 235012
  149.9 21.1 %copy-start.11 = (f32[18,18,64]{2,1,0:T(8,128)S(1)}, f32[18,18,64]{2,1,0:T(8,128)}, u32[]{:S(2)}) copy-start(f32[18,18,64]{2,1,0:T(8,128)} %get-tuple-element.40) | copy-start | bytes 248836
  151.2 5.4 %collective-permute-start.11 = (f32[2,5,8,64]{3,2,1,0:T(8,128)S(1)}, f32[2,5,8,64]{3,2,1,0:T(8,128)S(1)}, u32[]{:S(2)}, u32[]{:S(2)}) collective-permute-start(f32[2,5,8,64]{3,2,1,0:T(8,128)S(1)} %get-tuple-element.129), channel_id=1, source_target_pairs={{0,4},{4,8},{8,12},{12,16},{16,20},{20,24},{24,28},{1,5},{5,9},{9,... | collective-permute-start | bytes 61448 | tf_op jit(solution)/shard_map/ppermute | solution.py:26
  155.3 4.7 %collective-permute-start.12 = (f32[2,5,8,64]{3,2,1,0:T(8,128)S(1)}, f32[2,5,8,64]{3,2,1,0:T(8,128)S(1)}, u32[]{:S(2)}, u32[]{:S(2)}) collective-permute-start(f32[2,5,8,64]{3,2,1,0:T(8,128)S(1)} %get-tuple-element.130), channel_id=1, source_target_pairs={{4,0},{8,4},{12,8},{16,12},{20,16},{24,20},{28,24},{5,1},{9,5},{13... | collective-permute-start | bytes 61448 | tf_op jit(solution)/shard_map/ppermute | solution.py:26
  160.1 6.0 %collective-permute-start.13 = (f32[2,18,5,64]{3,2,1,0:T(8,128)S(1)}, f32[2,18,5,64]{3,2,1,0:T(8,128)S(1)}, u32[]{:S(2)}, u32[]{:S(2)}) collective-permute-start(f32[2,18,5,64]{3,2,1,0:T(8,128)S(1)} %get-tuple-element.85), channel_id=1, source_target_pairs={{0,1},{1,2},{2,3},{4,5},{5,6},{6,7},{8,9},{9,10},{10,11},{12,13},{... | collective-permute-start | bytes 138248 | tf_op jit(solution)/shard_map/ppermute | solution.py:26
  164.1 6.5 %collective-permute-start.14 = (f32[2,18,5,64]{3,2,1,0:T(8,128)S(1)}, f32[2,18,5,64]{3,2,1,0:T(8,128)S(1)}, u32[]{:S(2)}, u32[]{:S(2)}) collective-permute-start(f32[2,18,5,64]{3,2,1,0:T(8,128)S(1)} %get-tuple-element.86), channel_id=1, source_target_pairs={{1,0},{2,1},{3,2},{5,4},{6,5},{7,6},{9,8},{10,9},{11,10},{13,12},{... | collective-permute-start | bytes 138248 | tf_op jit(solution)/shard_map/ppermute | solution.py:26
  171.2 0.7 copy-start.19
  172.3 1.1 copy-start.1
  172.3 1.3 copy-start.9
